TPU v7x, 512 devices: a whole 4x4x16 slice. The times are simulated.
512 devices in a mesh: context: 128 (over z, y, core), tensor: 4 (over x).
Axes of the slice: x: 4, y: 4, z: 16, core: 2. Of those that a mesh axis runs over, the one named last changes fastest.
Arguments:
- projected: bfloat16 [3, 16, 512, 16384], P(None, 'tensor', None, 'context'), may hold values from -6 to 6
- long_filter: bfloat16 [512, 128], replicated, may hold values from -0.5 to 0.5
- cotangent: bfloat16 [16, 512, 16384], P('tensor', None, 'context'), may hold values from -6 to 6
Outputs:
- mixed: bfloat16 [16, 512, 16384], P('tensor', None, 'context')
- stream_grads: bfloat16 [3, 16, 512, 16384], P(None, 'tensor', None, 'context')
- filter_grads: float32 [512, 128], P('context')
All inputs are finite; a program needn't handle non-finite values.
Results may differ from a plain program's by a relative error of at most 0.0057.
Values may be sent and summed in bfloat16 or wider, within the bound.
No kernel may reach another device: no remote copies, remote signals or barrier semaphores. Data moves between devices by JAX's collectives and lax.ppermute only.
A program may use at most 64 MiB of HBM per device.

v0:
```python
import math

import jax
import jax.numpy as jnp
from jax import lax
from jax.sharding import PartitionSpec as P


def selector_table(filter_taps):
    rows = lax.broadcasted_iota(jnp.int32, (filter_taps, filter_taps), 0)
    cols = lax.broadcasted_iota(jnp.int32, (filter_taps, filter_taps), 1)
    offset = (rows - cols + filter_taps) % filter_taps
    taps = lax.broadcasted_iota(jnp.int32, (filter_taps, filter_taps, filter_taps), 0)
    table = (offset[None, :, :] == taps).astype(jnp.bfloat16)
    return (table.reshape(filter_taps, filter_taps * filter_taps), rows >= cols)


def conv_both(tiles, earlier, grad_tiles, grad_next, filters):
    groups, filter_taps = filters.shape
    block_width = math.gcd(groups, 32)
    table, lower = selector_table(filter_taps)
    table_wide = table.astype(jnp.float32)

    def advance(index, carry):
        circulant = jnp.dot(filters, table, preferred_element_type=jnp.float32).reshape(
            block_width, filter_taps, filter_taps
        )
        low_band = jnp.where(lower[None], circulant, 0.0).astype(jnp.bfloat16)
        high_band = jnp.where(lower[None], 0.0, circulant).astype(jnp.bfloat16)
        forward = jnp.einsum("mgbk,gik->mgbi", tiles, low_band, preferred_element_type=jnp.float32)
        forward = forward + jnp.einsum(
            "mgbk,gik->mgbi", earlier, high_band, preferred_element_type=jnp.float32
        )
        backward = jnp.einsum(
            "mgbi,gik->mgbk", grad_tiles, low_band, preferred_element_type=jnp.float32
        )
        backward = backward + jnp.einsum(
            "mgbi,gik->mgbk", grad_next, high_band, preferred_element_type=jnp.float32
        )
        outer_low = jnp.einsum(
            "mgbi,mgbk->gik", grad_tiles, tiles, preferred_element_type=jnp.float32
        )
        outer_high = jnp.einsum(
            "mgbi,mgbk->gik", grad_tiles, earlier, preferred_element_type=jnp.float32
        )
        merged = jnp.where(lower[None], outer_low, outer_high).reshape(
            block_width, filter_taps * filter_taps
        )
        sums = jnp.dot(merged, table_wide.T, precision=lax.Precision.HIGHEST)
        filtered_out = forward.astype(jnp.bfloat16)
        grads_out = backward.astype(jnp.bfloat16)
        return (filtered_out, grads_out, sums)

    initial = (
        jnp.zeros(tiles.shape, jnp.bfloat16),
        jnp.zeros(tiles.shape, jnp.bfloat16),
        jnp.zeros((groups, filter_taps), jnp.float32),
    )
    return lax.fori_loop(0, groups // block_width, advance, initial)


def shifted_tiles(tiles, before, grad_tiles, after):
    earlier = jnp.concatenate([before, tiles[:, :, :-1]], 2)
    grad_next = jnp.concatenate([grad_tiles[:, :, 1:], after], 2)
    return (earlier, grad_next)


def channel_filters(long_filter, own_groups):
    first_group = lax.axis_index("context") * own_groups
    return lax.dynamic_slice_in_dim(long_filter, first_group, own_groups, 0)


def channel_conv(columns, grad_columns, long_filter, filter_taps):
    members, own_groups, length = columns.shape
    filters = channel_filters(long_filter, own_groups)
    tiles = columns.reshape(members, own_groups, length // filter_taps, filter_taps)
    grad_tiles = grad_columns.reshape(members, own_groups, length // filter_taps, filter_taps)
    blank = jnp.zeros((members, own_groups, 1, filter_taps), jnp.bfloat16)
    earlier, grad_next = shifted_tiles(tiles, blank, grad_tiles, blank)
    filtered_tiles, gated_tiles, partial_taps = conv_both(
        tiles, earlier, grad_tiles, grad_next, filters
    )
    return (
        filtered_tiles.reshape(members, own_groups, length),
        gated_tiles.reshape(members, own_groups, length),
        partial_taps,
    )


def body(projected, long_filter, cotangent):
    filter_taps = long_filter.shape[1]
    query_stream = projected[0]
    key_stream = projected[1]
    value_stream = projected[2]
    gated = (key_stream.astype(jnp.float32) * value_stream.astype(jnp.float32)).astype(jnp.bfloat16)
    members, groups, local_tokens = gated.shape
    length = local_tokens * lax.axis_size("context")
    factor = 1.0 / math.sqrt(members * lax.axis_size("tensor") * length)
    grad_filtered = (cotangent.astype(jnp.float32) * query_stream.astype(jnp.float32)).astype(
        jnp.bfloat16
    )
    columns = lax.all_to_all(gated, "context", split_axis=1, concat_axis=2, tiled=True)
    grad_columns = lax.all_to_all(grad_filtered, "context", split_axis=1, concat_axis=2, tiled=True)
    filtered_columns, gated_columns, partial_taps = channel_conv(
        columns, grad_columns, long_filter, filter_taps
    )
    filtered = lax.all_to_all(filtered_columns, "context", split_axis=2, concat_axis=1, tiled=True)
    grad_gated = lax.all_to_all(gated_columns, "context", split_axis=2, concat_axis=1, tiled=True)
    filter_grads = lax.psum(partial_taps, "tensor") * factor
    filtered_wide = filtered.astype(jnp.float32)
    grad_wide = grad_gated.astype(jnp.float32)
    mixed = (query_stream.astype(jnp.float32) * filtered_wide).astype(jnp.bfloat16)
    stream_grads = jnp.stack(
        [
            cotangent.astype(jnp.float32) * filtered_wide,
            grad_wide * value_stream.astype(jnp.float32),
            grad_wide * key_stream.astype(jnp.float32),
        ]
    ).astype(jnp.bfloat16)
    return (mixed, stream_grads, filter_grads)


def solution(mesh):
    in_specs = (P(None, "tensor", None, "context"), P(), P("tensor", None, "context"))
    out_specs = (
        P("tensor", None, "context"),
        P(None, "tensor", None, "context"),
        P("context", None),
    )
    return jax.shard_map(body, mesh=mesh, in_specs=in_specs, out_specs=out_specs, check_vma=False)
```

profile of v0, /device:TPU:24, one launch (start us, length us, event | category | flops | bytes accessed | tf_op | source)
XLA Modules:
  0.0 418.1 jit_solution(2552468281968310351)
XLA Ops:
  0.6 2.3 fusion.32
  2.9 1.5 fusion.15
  4.4 19.3 %all-to-all-start = ((bf16[4,512,128]{2,0,1:T(4,128)(2,1)}), bf16[4,512,128]{2,0,1:T(4,128)(2,1)S(1)}, u32[]{:S(2)}, u32[]{:S(2)}) async-start(bf16[4,512,128]{2,0,1:T(4,128)(2,1)} %fusion.15), calls=%async_computation | async-start | bytes 1048576 | tf_op jit(solution)/shard_map/all_to_all | solution.py:102
  23.8 3.7 fusion.21
  27.8 28.9 %all-to-all-done = bf16[4,512,128]{2,0,1:T(4,128)(2,1)S(1)} async-done(((bf16[4,512,128]{2,0,1:T(4,128)(2,1)}), bf16[4,512,128]{2,0,1:T(4,128)(2,1)S(1)}, u32[]{:S(2)}, u32[]{:S(2)}) %all-to-all-start) | async-done | bytes 524320 | tf_op jit(solution)/shard_map/all_to_all | solution.py:102
  56.8 0.3 fusion.30
  57.1 0.4 fusion.7
  57.5 26.7 %copy.58 = bf16[4,4,128,128]{1,0,3,2:T(4,128)(2,1)} copy(bf16[4,4,128,128]{2,3,0,1:T(8,128)(2,1)S(1)} %fusion.7) | data formatting | bytes 1048576 | tf_op jit(solution)/shard_map/reshape | solution.py:84
  84.2 31.2 %reshape.98 = bf16[128,2,1024]{2,1,0:T(2,128)(2,1)S(1)} reshape(bf16[16384,4,4]{2,1,0:T(4,128)(2,1)} %bitcast.75) | data formatting | bytes 1048576
  115.4 39.7 %all_to_all.48 = bf16[128,2,1024]{2,1,0:T(2,128)(2,1)S(1)} all-to-all(bf16[128,2,1024]{2,1,0:T(2,128)(2,1)S(1)} %reshape.98), channel_id=1, replica_groups=mesh['context'=128,'tensor'=4] {'context'}, dimensions={0} | all-to-all | bytes 1048576 | tf_op jit(solution)/shard_map/all_to_all | solution.py:107
  155.1 37.0 %reshape.99 = bf16[16384,4,4]{2,1,0:T(4,128)(2,1)} reshape(bf16[128,2,1024]{2,1,0:T(2,128)(2,1)S(1)} %all_to_all.48) | data formatting | bytes 1048576
  192.2 21.7 %copy.29 = f32[4,4,128,128]{3,0,1,2:T(4,128)} copy(bf16[4,4,128,128]{1,0,3,2:T(4,128)(2,1)} %bitcast.76) | data formatting | bytes 1572864 | tf_op jit(solution)/shard_map/convert_element_type | solution.py:110
  213.8 3.2 fusion.12
  217.0 39.9 %all_to_all.49 = bf16[4,512,128]{2,0,1:T(4,128)(2,1)S(1)} all-to-all(bf16[4,512,128]{2,0,1:T(4,128)(2,1)S(1)} %get-tuple-element.32), channel_id=1, replica_groups=mesh['context'=128,'tensor'=4] {'context'}, dimensions={1} | all-to-all | bytes 1048576 | tf_op jit(solution)/shard_map/all_to_all | solution.py:103
  257.1 0.3 fusion.31
  257.4 0.1 slice.21
  257.5 0.3 fusion.6
  257.8 26.7 %copy.65 = bf16[4,4,128,128]{1,0,3,2:T(4,128)(2,1)} copy(bf16[4,4,128,128]{2,3,0,1:T(8,128)(2,1)S(1)} %fusion.6) | data formatting | bytes 1048576 | tf_op jit(solution)/shard_map/reshape | solution.py:85
  284.6 31.8 %reshape.100 = bf16[128,2,1024]{2,1,0:T(2,128)(2,1)} reshape(bf16[16384,4,4]{2,1,0:T(4,128)(2,1)} %bitcast.77) | data formatting | bytes 1048576
  316.4 7.0 %all-to-all-start.3 = ((bf16[128,2,1024]{2,1,0:T(2,128)(2,1)}), bf16[128,2,1024]{2,1,0:T(2,128)(2,1)S(1)}, u32[]{:S(2)}, u32[]{:S(2)}) async-start(bf16[128,2,1024]{2,1,0:T(2,128)(2,1)} %reshape.100), calls=%async_computation.3 | async-start | bytes 1048576 | tf_op jit(solution)/shard_map/all_to_all | solution.py:108
  323.4 1.9 copy.42
  325.3 0.4 convolution_bitcast_fusion
  325.7 0.3 convolution_bitcast_fusion.1
  326.0 4.1 fusion.8
  330.2 10.7 %psum.7 = f32[4,128]{1,0:T(4,128)S(1)} all-reduce(f32[4,128]{1,0:T(4,128)S(1)} %fusion.8), channel_id=1, replica_groups=mesh['context'=128,'tensor'=4] {'tensor'}, use_global_device_ids=true, to_apply=%region_0.1 | all-reduce | flops 512 | bytes 4096 | tf_op jit(solution)/shard_map/psum | solution.py:109
  340.9 0.6 broadcast_multiply_fusion
  341.5 14.9 %all-to-all-done.3 = bf16[128,2,1024]{2,1,0:T(2,128)(2,1)S(1)} async-done(((bf16[128,2,1024]{2,1,0:T(2,128)(2,1)}), bf16[128,2,1024]{2,1,0:T(2,128)(2,1)S(1)}, u32[]{:S(2)}, u32[]{:S(2)}) %all-to-all-start.3) | async-done | bytes 524320 | tf_op jit(solution)/shard_map/all_to_all | solution.py:108
  356.3 37.0 %reshape.101 = bf16[16384,4,4]{2,1,0:T(4,128)(2,1)} reshape(bf16[128,2,1024]{2,1,0:T(2,128)(2,1)S(1)} %all-to-all-done.3) | data formatting | bytes 1048576
  393.4 21.0 %copy.37 = f32[4,4,128,128]{3,0,1,2:T(4,128)S(1)} copy(bf16[4,4,128,128]{1,0,3,2:T(4,128)(2,1)} %bitcast.78) | data formatting | bytes 1572864 | tf_op jit(solution)/shard_map/convert_element_type | solution.py:111
  414.3 1.0 fusion.11
  415.4 1.3 pad_maximum_fusion
  416.7 1.4 copy.43
  (16 shorter events, 0.7 us)
Async XLA Ops:
  0.6 23.1 %copy-start = (bf16[512,128]{1,0:T(8,128)(2,1)S(1)}, bf16[512,128]{1,0:T(8,128)(2,1)}, u32[]{:S(2)}) copy-start(bf16[512,128]{1,0:T(8,128)(2,1)} %param.4) | copy-start | bytes 393220
  4.4 52.2 %all-to-all-start = ((bf16[4,512,128]{2,0,1:T(4,128)(2,1)}), bf16[4,512,128]{2,0,1:T(4,128)(2,1)S(1)}, u32[]{:S(2)}, u32[]{:S(2)}) async-start(bf16[4,512,128]{2,0,1:T(4,128)(2,1)} %fusion.15), calls=%async_computation | async-start | bytes 1048576 | tf_op jit(solution)/shard_map/all_to_all | solution.py:102
  192.2 21.7 %copy-start.2 = (bf16[1,4,512,128]{3,2,1,0:T(8,128)(2,1)S(1)}, bf16[1,4,512,128]{3,2,1,0:T(8,128)(2,1)}, u32[]{:S(2)}) copy-start(bf16[1,4,512,128]{3,2,1,0:T(8,128)(2,1)} %get-tuple-element.27) | copy-start | bytes 1572868
  192.2 21.7 %copy-start.4 = (bf16[4,512,128]{2,1,0:T(8,128)(2,1)S(1)}, bf16[4,512,128]{2,1,0:T(8,128)(2,1)}, u32[]{:S(2)}) copy-start(bf16[4,512,128]{2,1,0:T(8,128)(2,1)} %param.5) | copy-start | bytes 1572868
  316.4 39.9 %all-to-all-start.3 = ((bf16[128,2,1024]{2,1,0:T(2,128)(2,1)}), bf16[128,2,1024]{2,1,0:T(2,128)(2,1)S(1)}, u32[]{:S(2)}, u32[]{:S(2)}) async-start(bf16[128,2,1024]{2,1,0:T(2,128)(2,1)} %reshape.100), calls=%async_computation.3 | async-start | bytes 1048576 | tf_op jit(solution)/shard_map/all_to_all | solution.py:108
  414.3 1.0 copy-start.3
  415.4 2.7 copy-start.1
where the time goes:
time: 420 us; the launch traced here: 418 us
  local copies, waits for them, and re-layouts  239 us (57%)
  blocking collectives  90.3 us (22%)
  waiting for transfers between devices  43.8 us (10%)
  starting transfers between devices  26.3 us (6%)
  matrix products  9.88 us (2%)
  other arithmetic  7.57 us (2%)
    unnamed x16, local copies, waits for them, and re-layouts  140 us
    all_to_all x1, blocking collectives, body(): lax.all_to_all(grad_filtered, 'context', split_axis=1, concat_axis=2, til...  39.9 us
    all_to_all x1, blocking collectives, body(): lax.all_to_all(filtered_columns, 'context', split_axis=2, concat_axis=1,...  39.7 us
    all_to_all x1, waiting for transfers between devices, body(): lax.all_to_all(gated, 'context', split_axis=1, concat_axis=2, tiled=True)  28.9 us
    reshape x1, local copies, waits for them, and re-layouts, channel_conv(): filtered_tiles.reshape(members, own_groups, length)  26.7 us
    reshape x1, local copies, waits for them, and re-layouts, channel_conv(): gated_tiles.reshape(members, own_groups, length)  26.7 us
    convert_element_type x1, local copies, waits for them, and re-layouts, body(): filtered_wide = filtered.astype(jnp.float32)  21.7 us
    convert_element_type x1, local copies, waits for them, and re-layouts, body(): grad_wide = grad_gated.astype(jnp.float32)  21 us
  transfers between devices with their start and end apart: 2, of which 2 were waited for; matrix products, arithmetic and copies ran while one was open for 3% of the time, Pallas kernels for 0%

commit v1 on v0

v1 whole, which is shorter than its diff:
```python
import math

import jax
import jax.numpy as jnp
from jax import lax
from jax.sharding import PartitionSpec as P


def grouped_conv(lhs, rhs, groups):
    return lax.conv_general_dilated(
        lhs,
        rhs,
        window_strides=(1,),
        padding="VALID",
        dimension_numbers=("NCH", "OIH", "NCH"),
        feature_group_count=groups,
        preferred_element_type=jnp.float32,
    )


def body(projected, long_filter, cotangent):
    filter_taps = long_filter.shape[1]
    query_stream = projected[0]
    key_stream = projected[1]
    value_stream = projected[2]
    members, groups, local_tokens = key_stream.shape
    blocks = lax.axis_size("context")
    length = local_tokens * blocks
    factor = 1.0 / math.sqrt(members * lax.axis_size("tensor") * length)
    gated = (key_stream.astype(jnp.float32) * value_stream.astype(jnp.float32)).astype(jnp.bfloat16)
    grad_filtered = (cotangent.astype(jnp.float32) * query_stream.astype(jnp.float32)).astype(
        jnp.bfloat16
    )
    earlier = lax.ppermute(gated, "context", [(i, i + 1) for i in range(blocks - 1)])
    later = lax.ppermute(grad_filtered, "context", [(i + 1, i) for i in range(blocks - 1)])
    halo = filter_taps - 1
    gated_ext = jnp.concatenate([earlier[:, :, local_tokens - halo:], gated], 2)
    grad_ext = jnp.concatenate([grad_filtered, later[:, :, :halo]], 2)
    reversed_taps = long_filter[:, ::-1][:, None, :]
    filtered = grouped_conv(gated_ext, reversed_taps, groups).astype(jnp.bfloat16)
    grad_gated = grouped_conv(grad_ext, long_filter[:, None, :], groups).astype(jnp.bfloat16)
    tap_sums = lax.conv_general_dilated(
        gated_ext,
        grad_filtered,
        window_strides=(1,),
        padding=((0, 0),),
        dimension_numbers=lax.ConvDimensionNumbers((1, 0, 2), (1, 0, 2), (1, 0, 2)),
        batch_group_count=groups,
        preferred_element_type=jnp.float32,
    )
    partial_taps = tap_sums[:, 0, ::-1]
    own_taps = lax.psum_scatter(partial_taps, "context", scatter_dimension=0, tiled=True)
    filter_grads = lax.psum(own_taps, "tensor") * factor
    filtered_wide = filtered.astype(jnp.float32)
    grad_wide = grad_gated.astype(jnp.float32)
    mixed = (query_stream.astype(jnp.float32) * filtered_wide).astype(jnp.bfloat16)
    stream_grads = jnp.stack(
        [
            cotangent.astype(jnp.float32) * filtered_wide,
            grad_wide * value_stream.astype(jnp.float32),
            grad_wide * key_stream.astype(jnp.float32),
        ]
    ).astype(jnp.bfloat16)
    return (mixed, stream_grads, filter_grads)


def solution(mesh):
    in_specs = (P(None, "tensor", None, "context"), P(), P("tensor", None, "context"))
    out_specs = (
        P("tensor", None, "context"),
        P(None, "tensor", None, "context"),
        P("context", None),
    )
    return jax.shard_map(body, mesh=mesh, in_specs=in_specs, out_specs=out_specs, check_vma=False)
```

time: 420 us -> 448 us (1.067); the launches traced: 418 us -> 441 us
  waiting for transfers between devices: 43.8 us -> 336 us
  local copies, waits for them, and re-layouts: 239 us -> 12.5 us
  blocking collectives: 90.3 us -> 17.5 us
  matrix products: 9.88 us -> 53.9 us
  starting transfers between devices: 26.3 us -> 4.33 us
  between operations: 0.79 us -> 15.1 us
  other arithmetic: 7.57 us -> 1.59 us
    unnamed x0 -> x2, waiting for transfers between devices: none -> 329 us
    unnamed x16, local copies, waits for them, and re-layouts: 140 us -> 8.82 us
    all_to_all x2 -> x0, blocking collectives: 79.6 us -> none  [the longest x1 39.9 us: body(): lax.all_to_all(grad_filtered, 'context', split_axis=1, concat_axis=2, til...]
    conv_general_dilated x0 -> x3, matrix products: none -> 53.9 us  [the longest x2 29.4 us: grouped_conv(): lax.conv_general_dilated(lhs, rhs, window_strides=(1,), padding='VALID',...]
    reshape x2 -> x0, local copies, waits for them, and re-layouts: 53.4 us -> none  [the longest x1 26.7 us: channel_conv(): filtered_tiles.reshape(members, own_groups, length)]
    all_to_all x2 -> x0, waiting for transfers between devices: 43.8 us -> none  [the longest x1 28.9 us: body(): lax.all_to_all(gated, 'context', split_axis=1, concat_axis=2, tiled=True)]
    convert_element_type x4 -> x0, local copies, waits for them, and re-layouts: 42.9 us -> none  [the longest x1 21.7 us: body(): filtered_wide = filtered.astype(jnp.float32)]
    all_to_all x2 -> x0, starting transfers between devices: 26.3 us -> none  [the longest x1 19.3 us: body(): lax.all_to_all(gated, 'context', split_axis=1, concat_axis=2, tiled=True)]
  transfers between devices with their start and end apart: 2 -> 3, of which waited for: 2 -> 2; matrix products, arithmetic and copies ran while one was open for 3% -> 7% of each run, Pallas kernels for 0% -> 0%
where the time goes in v1:
time: 448 us; the launch traced here: 441 us
  waiting for transfers between devices  336 us (75%)
  matrix products  53.9 us (12%)
  blocking collectives  17.5 us (4%)
  between operations  15.1 us (3%)
  local copies, waits for them, and re-layouts  12.5 us (3%)
    unnamed x2, waiting for transfers between devices  329 us
    conv_general_dilated x2, matrix products, grouped_conv(): lax.conv_general_dilated(lhs, rhs, window_strides=(1,), padding='VALID',...  29.4 us
    conv_general_dilated x1, matrix products, body(): lax.conv_general_dilated(gated_ext, grad_filtered, window_strides=(1,), p...  24.5 us
    psum x1, blocking collectives, body(): filter_grads = lax.psum(own_taps, 'tensor') * factor  17.5 us
  transfers between devices with their start and end apart: 3, of which 2 were waited for; matrix products, arithmetic and copies ran while one was open for 7% of the time, Pallas kernels for 0%

profile of v1, /device:TPU:24, one launch (start us, length us, event | category | flops | bytes accessed | tf_op | source)
XLA Modules:
  0.0 441.3 jit_solution(13452718272975278500)
XLA Ops:
  7.2 0.0 all-reduce.3.cloned.1.call-start
  7.2 1.5 fusion.16
  8.7 0.4 copy.28
  9.1 0.0 copy-start
  9.1 0.0 copy-start.1
  9.1 0.4 copy.27
  9.5 0.3 fusion.4
  9.8 1.9 collective-permute-start
  11.7 0.4 rev.6
  12.1 0.2 copy.18
  12.3 0.4 copy.19
  12.7 0.4 copy.29
  13.2 7.2 %collective-permute-done = bf16[4,512,128]{1,0,2:T(4,128)(2,1)} collective-permute-done((bf16[4,512,128]{1,0,2:T(4,128)(2,1)S(1)}, bf16[4,512,128]{1,0,2:T(4,128)(2,1)}, u32[]{:S(2)}, u32[]{:S(2)}) %collective-permute-start) | collective-permute-done | bytes 524320 | tf_op jit(solution)/shard_map/ppermute | solution.py:34
  20.4 1.2 slice.20
  21.6 14.7 %fusion.11 = (bf16[1,4,512,128]{2,1,3,0:T(4,128)(2,1)}, bf16[4,512,128]{1,0,2:T(4,128)(2,1)}, bf16[4,512,128]{1,0,2:T(4,128)(2,1)S(1)}) fusion(bf16[4,512,128]{1,0,2:T(4,128)(2,1)S(1)} %copy.19, bf16[1,4,512,128]{2,1,3,0:T(4,128)(2,1)S(1)} %copy.29, bf16[512,1,128]{0,1,2:T(2,128)(2,1)S(1)} %copy.18, bf16[4,512,128]{1,0,2:T(4,128)(2,1)S(1)} %fusion.4, ...), kind=kOutput, calls=%fused_computation.21 | convolution fusion | flops 71819264 | bytes 3796992 | tf_op jit(solution)/shard_map/conv_general_dilated | solution.py:10
  36.3 2.4 collective-permute-start.1
  38.7 24.5 %fusion.12 = f32[512,1,128]{0,1,2:T(1,128)S(1)} fusion(bf16[4,512,128]{1,0,2:T(4,128)(2,1)} %get-tuple-element.13, bf16[4,512,128]{1,0,2:T(4,128)(2,1)S(1)} %fusion.4, bf16[4,512,127]{1,0,2:T(4,128)(2,1)S(1)} %slice.20), kind=kOutput, calls=%fused_computation.22 | convolution fusion | flops 69197824 | bytes 1830912 | tf_op jit(solution)/shard_map/conv_general_dilated | solution.py:42
  63.2 0.7 copy.31
  63.9 0.0 all-reduce.3.cloned.1.call-update
  63.9 0.2 copy.20
  64.1 1.3 dynamic-slice
  66.1 1.2 copy.21
  67.2 329.2 %all-reduce.3.cloned.1.call-done = f32[512,128]{0,1:T(8,128)} async-done(((f32[512,128]{0,1:T(8,128)}), f32[512,128]{0,1:T(8,128)}) %all-reduce.3.cloned.1.call-update) | async-done | bytes 262160
  396.4 0.9 constant_dynamic-slice_fusion
  397.3 17.5 %psum.7 = f32[4,128]{0,1:T(8,128)S(1)} all-reduce(f32[4,128]{0,1:T(8,128)S(1)} %constant_dynamic-slice_fusion), channel_id=1, replica_groups=mesh['context'=128,'tensor'=4] {'tensor'}, use_global_device_ids=true, to_apply=%region_1.0 | all-reduce | flops 512 | bytes 4096 | tf_op jit(solution)/shard_map/psum | solution.py:53
  414.8 0.7 copy.23
  415.5 0.0 collective-permute-done.1
  415.5 0.2 slice.21
  415.7 0.0 copy-start.2
  415.7 14.8 %fusion.10 = (bf16[1,4,512,128]{2,1,3,0:T(4,128)(2,1)S(1)}, bf16[1,4,512,128]{2,1,3,0:T(4,128)(2,1)S(1)}) fusion(bf16[1,4,512,128]{2,1,3,0:T(4,128)(2,1)S(1)} %copy.28, bf16[1,4,512,128]{2,1,3,0:T(4,128)(2,1)S(1)} %copy.27, bf16[512,1,128]{0,1,2:T(2,128)(2,1)S(1)} %copy.20, bf16[4,512,127]{1,0,2:T(4,128)(2,1)S(1)} %slice.21, ...), kind=kOutput, calls=%fused_computation.20 | convolution fusion | flops 71294976 | bytes 3272704 | tf_op jit(solution)/shard_map/conv_general_dilated | solution.py:10
  430.4 1.3 pad_maximum_fusion
  431.8 2.5 copy.22
  (5 shorter events, 0.1 us)
Async XLA Ops:
  7.2 389.3 %all-reduce.3.cloned.1.call-start = ((), (), s32[]{:S(2)}) async-start(), calls=%async_computation | async-start | bytes 524288
  9.1 2.6 copy-start
  9.1 3.2 copy-start.1
  9.8 10.6 %collective-permute-start = (bf16[4,512,128]{1,0,2:T(4,128)(2,1)S(1)}, bf16[4,512,128]{1,0,2:T(4,128)(2,1)}, u32[]{:S(2)}, u32[]{:S(2)}) collective-permute-start(bf16[4,512,128]{1,0,2:T(4,128)(2,1)S(1)} %fusion.4), channel_id=1, source_target_pairs={{0,4},{4,8},{8,12},{12,16},{16,20},{20,24},{24,28},{28,32},{32,36}... | collective-permute-start | bytes 1572872 | tf_op jit(solution)/shard_map/ppermute | solution.py:34
  36.3 379.2 %collective-permute-start.1 = (bf16[4,512,128]{1,0,2:T(4,128)(2,1)}, bf16[4,512,128]{1,0,2:T(4,128)(2,1)S(1)}, u32[]{:S(2)}, u32[]{:S(2)}) collective-permute-start(bf16[4,512,128]{1,0,2:T(4,128)(2,1)} %get-tuple-element.13), channel_id=1, source_target_pairs={{4,0},{8,4},{12,8},{16,12},{20,16},{24,20},{28,24},{32,28},{36,32}... | collective-permute-start | bytes 1572872 | tf_op jit(solution)/shard_map/ppermute | solution.py:35
  415.7 14.8 %copy-start.2 = (bf16[1,4,512,128]{2,1,3,0:T(4,128)(2,1)S(1)}, bf16[1,4,512,128]{2,1,3,0:T(4,128)(2,1)}, u32[]{:S(2)}) copy-start(bf16[1,4,512,128]{2,1,3,0:T(4,128)(2,1)} %get-tuple-element.12) | copy-start | bytes 1572868
Sparse Core Ops, SparseCore 0:
  64.1 332.3 all-reduce.2
